TPU v7x, 512 devices: a whole 4x8x8 slice. The times are simulated.
512 devices in a mesh: fsdp: 128 (over z, y, core), tp: 4 (over x).
Axes of the slice: x: 4, y: 8, z: 8, core: 2. Of those that a mesh axis runs over, the one named last changes fastest.
Arguments:
- q_grad: bfloat16 [128, 1280, 768], P('fsdp', None, 'tp'), may hold values from -24 to 24, as said below
- o_grad: bfloat16 [128, 768, 1280], P('fsdp', 'tp'), may hold values from -24 to 24, as said below
- norm_grad: float32 [128, 4, 1344], P('fsdp', 'tp'), may hold values from -6 to 6, as said below
- emb_grad: bfloat16 [8192, 1280], P('fsdp', 'tp'), may hold values from -6 to 6, as said below
- flat_master: float32 [4, 491520], P('tp', 'fsdp'), may hold values from -0.15625 to 0.15625
- flat_first: float32 [4, 491520], P('tp', 'fsdp'), may hold values from -0.75 to 0.75
- flat_second: float32 [4, 491520], P('tp', 'fsdp'), may hold values from 0.001 to 0.1
- emb_master: float32 [8192, 1280], P(('fsdp', 'tp')), may hold values from -0.3125 to 0.3125
- emb_first: float32 [8192, 1280], P(('fsdp', 'tp')), may hold values from -0.75 to 0.75
- emb_second: float32 [8192, 1280], P(('fsdp', 'tp')), may hold values from 0.001 to 0.1
- norm_master: float32 [1344], replicated, may hold values from 0.5 to 1.5
- norm_first: float32 [1344], replicated, may hold values from -0.75 to 0.75
- norm_second: float32 [1344], replicated, may hold values from 0.001 to 0.1
- step_count: int32 [1], replicated, may hold values from 1 to 64
Outputs:
- new_flat_master: float32 [4, 491520], P('tp', 'fsdp')
- new_flat_first: float32 [4, 491520], P('tp', 'fsdp')
- new_flat_second: float32 [4, 491520], P('tp', 'fsdp')
- new_emb_master: float32 [8192, 1280], P(('fsdp', 'tp'))
- new_emb_first: float32 [8192, 1280], P(('fsdp', 'tp'))
- new_emb_second: float32 [8192, 1280], P(('fsdp', 'tp'))
- new_norm_master: float32 [1344], replicated
- new_norm_first: float32 [1344], replicated
- new_norm_second: float32 [1344], replicated
- q_weight: bfloat16 [1280, 768], P(None, 'tp')
- o_weight: bfloat16 [768, 1280], P('tp')
- q_average: bfloat16 [1280, 768], P('fsdp')
- o_average: bfloat16 [768, 1280], P(None, 'fsdp')
- emb_weight: bfloat16 [8192, 1280], P('fsdp', 'tp')
Inputs may be any that keep to these rules, and one draw needn't show every extreme that they name: `q_grad`: each data replica's gradient of the query projection. `o_grad`: each data replica's gradient of the output projection. `norm_grad`: each device's gradient of the gains. `emb_grad`: the embedding slice's summed gradient.
All inputs are finite; a program needn't handle non-finite values.
Results may differ from a plain program's by a relative error of at most 0.0004.
Values may be sent and summed in bfloat16 or wider, within the bound.
No kernel may reach another device: no remote copies, remote signals or barrier semaphores. Data moves between devices by JAX's collectives and lax.ppermute only.
A program may use at most 64 MiB of HBM per device.

v0:
```python
import math
import jax
import jax.numpy as jnp
from jax import lax
from jax.sharding import PartitionSpec as P

BETA_ONE = 0.9
BETA_TWO = 0.95
EPSILON = 1e-08
LEARN_RATE = 0.0053


def adam_update(weights_in, first_in, second_in, gradient, first_fix, second_fix, decay_rate):
    first_out = BETA_ONE * first_in + (1.0 - BETA_ONE) * gradient
    second_out = BETA_TWO * second_in + (1.0 - BETA_TWO) * gradient * gradient
    update = first_out / first_fix / (jnp.sqrt(second_out / second_fix) + EPSILON)
    weights_out = weights_in - LEARN_RATE * (update + decay_rate * weights_in)
    return (weights_out, first_out, second_out)


def body(
    q_grad,
    o_grad,
    norm_grad,
    emb_grad,
    flat_master,
    flat_first,
    flat_second,
    emb_master,
    emb_first,
    emb_second,
    norm_master,
    norm_first,
    norm_second,
    step_count,
):
    fsdp_count = lax.axis_size("fsdp")
    tp_count = lax.axis_size("tp")
    width = q_grad.shape[1]
    q_columns = q_grad.shape[2]
    entry_count = (
        2 * width * q_columns * tp_count
        + emb_grad.shape[0] * fsdp_count * width
        + norm_master.shape[0]
    )
    clip_limit = 0.5 * math.sqrt(entry_count)
    local_flat = jnp.concatenate([q_grad[0].reshape(-1), o_grad[0].reshape(-1)])
    piece_len = local_flat.shape[0] // fsdp_count
    summed = lax.psum(local_flat.astype(jnp.float32), "fsdp")
    grad_piece = lax.dynamic_slice_in_dim(summed, lax.axis_index("fsdp") * piece_len, piece_len, 0)
    emb_piece = lax.all_to_all(emb_grad, "tp", split_axis=0, concat_axis=1, tiled=True).astype(
        jnp.float32
    )
    local_squares = jnp.sum(grad_piece * grad_piece) + jnp.sum(emb_piece * emb_piece)
    gains_local = norm_grad[0, 0]
    gain_sum = lax.psum(gains_local, ("fsdp", "tp"))
    global_squares = lax.psum(local_squares, ("fsdp", "tp"))
    grad_norm = jnp.sqrt(global_squares + jnp.sum(gain_sum * gain_sum))
    clip_factor = jnp.minimum(jnp.float32(1.0), clip_limit / (grad_norm + 1e-06))
    step_value = step_count[0].astype(jnp.float32)
    first_fix = 1.0 - jnp.power(jnp.float32(BETA_ONE), step_value)
    second_fix = 1.0 - jnp.power(jnp.float32(BETA_TWO), step_value)
    flat_new, flat_one, flat_two = adam_update(
        flat_master[0],
        flat_first[0],
        flat_second[0],
        clip_factor * grad_piece,
        first_fix,
        second_fix,
        0.1,
    )
    emb_new, emb_one, emb_two = adam_update(
        emb_master, emb_first, emb_second, clip_factor * emb_piece, first_fix, second_fix, 0.1
    )
    norm_new, norm_one, norm_two = adam_update(
        norm_master, norm_first, norm_second, clip_factor * gain_sum, first_fix, second_fix, 0.0
    )
    gathered = lax.all_gather(flat_new.astype(jnp.bfloat16), "fsdp", axis=0, tiled=True)
    q_weight = gathered[: width * q_columns].reshape(width, q_columns)
    o_weight = gathered[width * q_columns :].reshape(q_columns, width)
    block_rows = width // fsdp_count
    block_start = lax.axis_index("fsdp") * block_rows
    q_block = lax.dynamic_slice_in_dim(q_weight, block_start, block_rows, 0)
    o_block = lax.dynamic_slice_in_dim(o_weight, block_start, block_rows, 1)
    q_average, o_average = (
        lax.all_gather(q_block, "tp", axis=1, tiled=True),
        lax.all_gather(o_block, "tp", axis=0, tiled=True),
    )
    emb_weight = lax.all_to_all(
        emb_new.astype(jnp.bfloat16), "tp", split_axis=1, concat_axis=0, tiled=True
    )
    return (
        flat_new[None, :],
        flat_one[None, :],
        flat_two[None, :],
        emb_new,
        emb_one,
        emb_two,
        norm_new,
        norm_one,
        norm_two,
        q_weight,
        o_weight,
        q_average,
        o_average,
        emb_weight,
    )


def solution(mesh):
    return jax.shard_map(
        body,
        mesh=mesh,
        in_specs=(
            P("fsdp", None, "tp"),
            P("fsdp", "tp", None),
            P("fsdp", "tp", None),
            P("fsdp", "tp"),
            P("tp", "fsdp"),
            P("tp", "fsdp"),
            P("tp", "fsdp"),
            P(("fsdp", "tp"), None),
            P(("fsdp", "tp"), None),
            P(("fsdp", "tp"), None),
            P(),
            P(),
            P(),
            P(),
        ),
        out_specs=(
            P("tp", "fsdp"),
            P("tp", "fsdp"),
            P("tp", "fsdp"),
            P(("fsdp", "tp"), None),
            P(("fsdp", "tp"), None),
            P(("fsdp", "tp"), None),
            P(),
            P(),
            P(),
            P(None, "tp"),
            P("tp", None),
            P("fsdp", None),
            P(None, "fsdp"),
            P("fsdp", "tp"),
        ),
        check_vma=False,
    )
```

profile of v0, /device:TPU:24, one launch (start us, length us, event | category | flops | bytes accessed | tf_op | source)
XLA Modules:
  0.0 419.8 jit_solution(9161934839932907746)
XLA Ops:
  7.2 0.0 all-reduce.3.cloned.1.call-start
  7.2 1.3 copy.56
  8.6 0.8 reshape_squeeze.6
  9.3 0.6 reshape_squeeze.7
  9.9 0.0 copy-start.6
  9.9 0.0 copy-start.7
  10.0 0.0 copy-start.11
  10.0 0.0 copy-start.5
  10.0 1.4 maximum_convert_fusion
  11.4 0.0 all-reduce.3.cloned.1.call-update
  11.4 4.3 %all-to-all-start = ((bf16[4,16,320]{2,1,0:T(8,128)(2,1)}), bf16[4,16,320]{2,1,0:T(8,128)(2,1)S(1)}, u32[]{:S(2)}, u32[]{:S(2)}) async-start(bf16[4,16,320]{2,1,0:T(8,128)(2,1)} %bitcast), calls=%async_computation | async-start | bytes 98304 | tf_op jit(solution)/shard_map/all_to_all | solution.py:51
  15.7 0.1 multiply_reduce_fusion.1
  16.7 4.6 %all-to-all-done = bf16[4,16,320]{2,1,0:T(8,128)(2,1)S(1)} async-done(((bf16[4,16,320]{2,1,0:T(8,128)(2,1)}), bf16[4,16,320]{2,1,0:T(8,128)(2,1)S(1)}, u32[]{:S(2)}, u32[]{:S(2)}) %all-to-all-start) | async-done | bytes 40992 | tf_op jit(solution)/shard_map/all_to_all | solution.py:51
  21.3 0.6 fusion
  21.9 197.6 %all-reduce.3.cloned.1.call-done = f32[491520]{0:T(1024)} async-done(((f32[491520]{0:T(1024)}), f32[491520]{0:T(1024)}) %all-reduce.3.cloned.1.call-update) | async-done | bytes 1966096 | tf_op jit(solution)/shard_map/psum | solution.py:49
  219.5 1.4 multiply_reduce_fusion
  222.2 95.9 %all-reduce = (f32[]{:T(128)}, f32[1344]{0:T(1024)S(1)}) all-reduce(f32[]{:T(128)S(6)} %add.68, f32[1344]{0:T(1024)S(1)} %reduce.4), channel_id=1, replica_groups=mesh['fsdp'=128,'tp'=4] {'fsdp','tp'}, use_global_device_ids=true, to_apply=%region_3.0 | all-reduce | flops 1345 | bytes 10760 | tf_op jit(solution)/shard_map/psum | solution.py:57
  318.1 0.6 multiply_reduce_fusion.3
  320.1 0.8 fusion.7
  321.0 51.2 %all-gather = bf16[128,1,3840]{2,1,0:T(2,128)(2,1)S(1)} all-gather(bf16[1,1,3840]{2,1,0:T(2,128)(2,1)S(1)} %reshape.68), channel_id=1, replica_groups=mesh['fsdp'=128,'tp'=4] {'fsdp'}, dimensions={0}, use_global_device_ids=true | all-gather | bytes 990720 | tf_op jit(solution)/shard_map/all_gather | solution.py:78
  372.2 4.3 %slice_reduce_fusion = (bf16[64,3840]{1,0:T(8,128)(2,1)S(1)}, bf16[64,3840]{1,0:T(8,128)(2,1)S(1)}) fusion(bf16[128,1,3840]{2,1,0:T(2,128)(2,1)S(1)} %all-gather), kind=kLoop, calls=%fused_computation | loop fusion | bytes 1966080 | tf_op jit(solution)/shard_map/slice | solution.py:80
  376.4 0.0 copy-start.2
  376.5 0.0 copy-start.3
  376.5 0.0 copy-start.4
  376.5 0.0 copy-start.8
  376.5 0.0 copy-start.9
  376.5 0.0 copy-start.10
  376.5 0.8 slice.27
  377.3 0.2 slice.29
  377.6 0.0 copy-start
  377.6 0.1 mul.176
  377.8 0.7 fusion.5
  378.5 0.1 all_to_all.26
  378.6 0.6 copy.61
  379.3 3.3 all-to-all-start.1
  382.5 0.1 constant_dynamic-slice_fusion
  382.7 0.6 multiply_subtract_fusion.2
  383.3 1.0 copy.62
  384.3 12.7 %all-gather.1 = bf16[4,192,10]{1,2,0:T(8,128)(2,1)S(1)} all-gather(bf16[1,192,10]{1,2,0:T(8,128)(2,1)S(1)} %dynamic-slice_bitcast_fusion), channel_id=1, replica_groups=mesh['fsdp'=128,'tp'=4] {'tp'}, dimensions={0}, use_global_device_ids=true | all-gather | bytes 19200 | tf_op jit(solution)/shard_map/all_gather | solution.py:86
  397.1 0.7 reshape.71
  397.8 0.1 copy.59
  397.8 11.9 %all-gather.2 = bf16[4,192,10]{1,2,0:T(8,128)(2,1)S(1)} all-gather(bf16[1,192,10]{1,2,0:T(8,128)(2,1)S(1)} %bitcast.19), channel_id=1, replica_groups=mesh['fsdp'=128,'tp'=4] {'tp'}, dimensions={0}, use_global_device_ids=true | all-gather | bytes 19200 | tf_op jit(solution)/shard_map/all_gather | solution.py:87
  409.8 0.7 reshape.73
  410.5 0.6 broadcast_in_dim.10
  411.1 0.6 broadcast_in_dim.11
  411.7 0.6 broadcast_in_dim.9
  412.3 0.0 all-to-all-done.1
  412.3 0.6 copy.66
  (21 shorter events, 0.2 us)
Async XLA Ops:
  7.2 2.2 copy-start.1
  7.2 212.3 %all-reduce.3.cloned.1.call-start = ((), (), s32[]{:S(2)}) async-start(), calls=%async_computation.2 | async-start | bytes 3932160 | tf_op jit(solution)/shard_map/psum | solution.py:49
  9.9 5.8 %copy-start.6 = (f32[1,3840]{1,0:T(1,128)S(1)}, f32[1,3840]{1,0:T(1,128)}, u32[]{:S(2)}) copy-start(f32[1,3840]{1,0:T(1,128)} %param.20) | copy-start | bytes 46084
  9.9 5.8 %copy-start.7 = (f32[1,3840]{1,0:T(1,128)S(1)}, f32[1,3840]{1,0:T(1,128)}, u32[]{:S(2)}) copy-start(f32[1,3840]{1,0:T(1,128)} %param.19) | copy-start | bytes 46084
  10.0 6.6 %copy-start.11 = (f32[1,1,1344]{2,1,0:T(1,128)S(1)}, f32[1,1,1344]{2,1,0:T(1,128)}, u32[]{:S(2)}) copy-start(f32[1,1,1344]{2,1,0:T(1,128)} %param.16) | copy-start | bytes 16132
  10.0 6.6 %copy-start.5 = (f32[1,3840]{1,0:T(1,128)S(1)}, f32[1,3840]{1,0:T(1,128)}, u32[]{:S(2)}) copy-start(f32[1,3840]{1,0:T(1,128)} %param.18) | copy-start | bytes 46084
  11.4 9.8 %all-to-all-start = ((bf16[4,16,320]{2,1,0:T(8,128)(2,1)}), bf16[4,16,320]{2,1,0:T(8,128)(2,1)S(1)}, u32[]{:S(2)}, u32[]{:S(2)}) async-start(bf16[4,16,320]{2,1,0:T(8,128)(2,1)} %bitcast), calls=%async_computation | async-start | bytes 98304 | tf_op jit(solution)/shard_map/all_to_all | solution.py:51
  376.4 1.3 copy-start.2
  376.5 1.3 copy-start.3
  376.5 1.3 copy-start.4
  376.5 6.2 %copy-start.8 = (f32[1344]{0:T(1024)S(1)}, f32[1344]{0:T(1024)}, u32[]{:S(2)}) copy-start(f32[1344]{0:T(1024)} %param.24) | copy-start | bytes 16132
  376.5 6.2 %copy-start.9 = (f32[1344]{0:T(1024)S(1)}, f32[1344]{0:T(1024)}, u32[]{:S(2)}) copy-start(f32[1344]{0:T(1024)} %param.26) | copy-start | bytes 16132
  376.5 6.2 %copy-start.10 = (f32[1344]{0:T(1024)S(1)}, f32[1344]{0:T(1024)}, u32[]{:S(2)}) copy-start(f32[1344]{0:T(1024)} %param.25) | copy-start | bytes 16132
  377.6 35.4 %copy-start = (bf16[192,1280]{1,0:T(8,128)(2,1)}, bf16[192,1280]{1,0:T(8,128)(2,1)S(1)}, u32[]{:S(2)}) copy-start(bf16[192,1280]{1,0:T(8,128)(2,1)S(1)} %slice.29) | copy-start | bytes 1474564
  379.3 33.1 %all-to-all-start.1 = ((bf16[16,4,320]{2,0,1:T(8,128)(2,1)}), bf16[16,4,320]{2,0,1:T(8,128)(2,1)S(1)}, u32[]{:S(2)}, u32[]{:S(2)}) async-start(bf16[16,4,320]{2,0,1:T(8,128)(2,1)} %copy.61), calls=%async_computation.1 | async-start | bytes 98304 | tf_op jit(solution)/shard_map/all_to_all | solution.py:89
Sparse Core Ops, SparseCore 0:
  11.5 207.9 all-reduce.2
where the time goes:
time: 420 us
  waiting for transfers between devices  202 us (48%)
  blocking collectives  172 us (41%)
  between operations  17.7 us (4%)
  local copies, waits for them, and re-layouts  14 us (3%)
  starting transfers between devices  7.62 us (2%)
  other arithmetic  6.4 us (2%)
    psum x1, waiting for transfers between devices, body(): summed = lax.psum(local_flat.astype(jnp.float32), 'fsdp')  198 us
    psum x1, blocking collectives, body(): global_squares = lax.psum(local_squares, ('fsdp', 'tp'))  95.9 us
    all_gather x1, blocking collectives, body(): lax.all_gather(flat_new.astype(jnp.bfloat16), 'fsdp', axis=0, tiled=True)  51.2 us
    all_gather x1, blocking collectives, body(): lax.all_gather(q_block, 'tp', axis=1, tiled=True)  12.7 us
    all_gather x1, blocking collectives, body(): lax.all_gather(o_block, 'tp', axis=0, tiled=True)  11.9 us
  transfers between devices with their start and end apart: 3, of which 2 were waited for; matrix products, arithmetic and copies ran while one was open for 1% of the time, Pallas kernels for 0%

commit v1 on v0

--- a/solution.py
+++ b/solution.py
@@ -8,6 +8,11 @@
 BETA_TWO = 0.95
 EPSILON = 1e-08
 LEARN_RATE = 0.0053
+
+
+def swapped_in(x, axis, along):
+    repeated = jnp.stack([x] * lax.axis_size(axis))
+    return jnp.concatenate(lax.all_to_all(repeated, axis, 0, 0), axis=along)
 
 
 def adam_update(weights_in, first_in, second_in, gradient, first_fix, second_fix, decay_rate):
@@ -84,7 +89,7 @@
     o_block = lax.dynamic_slice_in_dim(o_weight, block_start, block_rows, 1)
     q_average, o_average = (
         lax.all_gather(q_block, "tp", axis=1, tiled=True),
-        lax.all_gather(o_block, "tp", axis=0, tiled=True),
+        swapped_in(o_block, "tp", 0),
     )
     emb_weight = lax.all_to_all(
         emb_new.astype(jnp.bfloat16), "tp", split_axis=1, concat_axis=0, tiled=True

time: 420 us -> 415 us (0.988)
  blocking collectives: 172 us -> 160 us
    all_gather x1 -> x0, blocking collectives: 11.9 us -> none  [body(): lax.all_gather(o_block, 'tp', axis=0, tiled=True)]
  transfers between devices with their start and end apart: 3 -> 4, of which waited for: 2 -> 3; matrix products, arithmetic and copies ran while one was open for 1% -> 2% of each run, Pallas kernels for 0% -> 0%
where the time goes in v1:
time: 415 us; the launch traced here: 414 us
  waiting for transfers between devices  204 us (49%)
  blocking collectives  160 us (39%)
  between operations  17.7 us (4%)
  local copies, waits for them, and re-layouts  14.8 us (4%)
  starting transfers between devices  10.9 us (3%)
  other arithmetic  6.39 us (2%)
    psum x1, waiting for transfers between devices, body(): summed = lax.psum(local_flat.astype(jnp.float32), 'fsdp')  198 us
    psum x1, blocking collectives, body(): global_squares = lax.psum(local_squares, ('fsdp', 'tp'))  95.9 us
    all_gather x1, blocking collectives, body(): lax.all_gather(flat_new.astype(jnp.bfloat16), 'fsdp', axis=0, tiled=True)  51.2 us
    all_gather x1, blocking collectives, body(): lax.all_gather(q_block, 'tp', axis=1, tiled=True)  12.7 us
  transfers between devices with their start and end apart: 4, of which 3 were waited for; matrix products, arithmetic and copies ran while one was open for 2% of the time, Pallas kernels for 0%

profile of v1, /device:TPU:24, one launch (start us, length us, event | category | flops | bytes accessed | tf_op | source)
XLA Modules:
  0.0 414.1 jit_solution(1278587095123389375)
XLA Ops:
  7.2 0.0 all-reduce.3.cloned.1.call-start
  7.2 1.3 copy.55
  8.6 0.8 reshape_squeeze.6
  9.3 0.6 reshape_squeeze.7
  9.9 0.0 copy-start.6
  9.9 0.0 copy-start.7
  10.0 0.0 copy-start.11
  10.0 0.0 copy-start.5
  10.0 1.4 maximum_convert_fusion
  11.4 0.0 all-reduce.3.cloned.1.call-update
  11.4 4.3 %all-to-all-start = ((bf16[4,16,320]{2,1,0:T(8,128)(2,1)}), bf16[4,16,320]{2,1,0:T(8,128)(2,1)S(1)}, u32[]{:S(2)}, u32[]{:S(2)}) async-start(bf16[4,16,320]{2,1,0:T(8,128)(2,1)} %bitcast), calls=%async_computation | async-start | bytes 98304 | tf_op jit(solution)/shard_map/all_to_all | solution.py:56
  15.7 0.1 multiply_reduce_fusion.1
  16.7 4.6 %all-to-all-done = bf16[4,16,320]{2,1,0:T(8,128)(2,1)S(1)} async-done(((bf16[4,16,320]{2,1,0:T(8,128)(2,1)}), bf16[4,16,320]{2,1,0:T(8,128)(2,1)S(1)}, u32[]{:S(2)}, u32[]{:S(2)}) %all-to-all-start) | async-done | bytes 40992 | tf_op jit(solution)/shard_map/all_to_all | solution.py:56
  21.3 0.6 fusion
  21.9 197.6 %all-reduce.3.cloned.1.call-done = f32[491520]{0:T(1024)} async-done(((f32[491520]{0:T(1024)}), f32[491520]{0:T(1024)}) %all-reduce.3.cloned.1.call-update) | async-done | bytes 1966096 | tf_op jit(solution)/shard_map/psum | solution.py:54
  219.5 1.4 multiply_reduce_fusion
  222.2 95.9 %all-reduce = (f32[]{:T(128)}, f32[1344]{0:T(1024)S(1)}) all-reduce(f32[]{:T(128)S(6)} %add.68, f32[1344]{0:T(1024)S(1)} %reduce.4), channel_id=1, replica_groups=mesh['fsdp'=128,'tp'=4] {'fsdp','tp'}, use_global_device_ids=true, to_apply=%region_3.0 | all-reduce | flops 1345 | bytes 10760 | tf_op jit(solution)/shard_map/psum | solution.py:62
  318.1 0.6 multiply_reduce_fusion.3
  320.1 0.8 fusion.7
  321.0 51.2 %all-gather = bf16[128,1,3840]{2,1,0:T(2,128)(2,1)S(1)} all-gather(bf16[1,1,3840]{2,1,0:T(2,128)(2,1)S(1)} %reshape.74), channel_id=1, replica_groups=mesh['fsdp'=128,'tp'=4] {'fsdp'}, dimensions={0}, use_global_device_ids=true | all-gather | bytes 990720 | tf_op jit(solution)/shard_map/all_gather | solution.py:83
  372.2 0.0 copy-start.10
  372.2 4.3 %slice_reduce_fusion = (bf16[64,3840]{1,0:T(8,128)(2,1)S(1)}, bf16[64,3840]{1,0:T(8,128)(2,1)S(1)}) fusion(bf16[128,1,3840]{2,1,0:T(2,128)(2,1)S(1)} %all-gather), kind=kLoop, calls=%fused_computation | loop fusion | bytes 1966080 | tf_op jit(solution)/shard_map/slice | solution.py:85
  376.5 0.2 slice.29
  376.7 0.0 copy-start
  376.7 0.1 constant_dynamic-slice_fusion
  376.8 0.1 copy.58
  376.9 0.7 reshape.88
  377.7 3.3 all-to-all-start.1
  381.0 0.1 mul.176
  381.1 0.7 fusion.5
  381.8 0.0 copy-done.10
  381.9 0.6 multiply_subtract_fusion.2
  382.5 0.8 slice.27
  383.3 0.1 all_to_all.30
  383.4 0.6 copy.60
  384.0 2.2 all-to-all-done.1
  386.2 3.3 all-to-all-start.2
  389.6 1.0 copy.61
  390.6 0.0 copy-done
  390.6 12.7 %all-gather.1 = bf16[4,192,10]{1,2,0:T(8,128)(2,1)S(1)} all-gather(bf16[1,192,10]{1,2,0:T(8,128)(2,1)S(1)} %dynamic-slice_bitcast_fusion), channel_id=1, replica_groups=mesh['fsdp'=128,'tp'=4] {'tp'}, dimensions={0}, use_global_device_ids=true | all-gather | bytes 19200 | tf_op jit(solution)/shard_map/all_gather | solution.py:91
  403.3 0.7 reshape.77
  404.0 0.6 broadcast_in_dim.10
  404.6 0.6 broadcast_in_dim.11
  405.2 0.6 broadcast_in_dim.9
  405.8 0.1 reshape.89
  405.9 0.7 reshape.73
  406.6 0.0 all-to-all-done.2
  406.7 0.6 copy.65
  (25 shorter events, 0.2 us)
Async XLA Ops:
  7.2 2.2 copy-start.1
  7.2 212.3 %all-reduce.3.cloned.1.call-start = ((), (), s32[]{:S(2)}) async-start(), calls=%async_computation.3 | async-start | bytes 3932160 | tf_op jit(solution)/shard_map/psum | solution.py:54
  9.9 5.8 %copy-start.6 = (f32[1,3840]{1,0:T(1,128)S(1)}, f32[1,3840]{1,0:T(1,128)}, u32[]{:S(2)}) copy-start(f32[1,3840]{1,0:T(1,128)} %param.20) | copy-start | bytes 46084
  9.9 5.8 %copy-start.7 = (f32[1,3840]{1,0:T(1,128)S(1)}, f32[1,3840]{1,0:T(1,128)}, u32[]{:S(2)}) copy-start(f32[1,3840]{1,0:T(1,128)} %param.19) | copy-start | bytes 46084
  10.0 6.6 %copy-start.11 = (f32[1,1,1344]{2,1,0:T(1,128)S(1)}, f32[1,1,1344]{2,1,0:T(1,128)}, u32[]{:S(2)}) copy-start(f32[1,1,1344]{2,1,0:T(1,128)} %param.16) | copy-start | bytes 16132
  10.0 6.6 %copy-start.5 = (f32[1,3840]{1,0:T(1,128)S(1)}, f32[1,3840]{1,0:T(1,128)}, u32[]{:S(2)}) copy-start(f32[1,3840]{1,0:T(1,128)} %param.18) | copy-start | bytes 46084
  11.4 9.8 %all-to-all-start = ((bf16[4,16,320]{2,1,0:T(8,128)(2,1)}), bf16[4,16,320]{2,1,0:T(8,128)(2,1)S(1)}, u32[]{:S(2)}, u32[]{:S(2)}) async-start(bf16[4,16,320]{2,1,0:T(8,128)(2,1)} %bitcast), calls=%async_computation | async-start | bytes 98304 | tf_op jit(solution)/shard_map/all_to_all | solution.py:56
  372.2 8.9 %copy-start.2 = (f32[16,1280]{1,0:T(8,128)S(1)}, f32[16,1280]{1,0:T(8,128)}, u32[]{:S(2)}) copy-start(f32[16,1280]{1,0:T(8,128)} %param.21) | copy-start | bytes 245764
  372.2 8.9 %copy-start.3 = (f32[16,1280]{1,0:T(8,128)S(1)}, f32[16,1280]{1,0:T(8,128)}, u32[]{:S(2)}) copy-start(f32[16,1280]{1,0:T(8,128)} %param.23) | copy-start | bytes 245764
  372.2 8.9 %copy-start.4 = (f32[16,1280]{1,0:T(8,128)S(1)}, f32[16,1280]{1,0:T(8,128)}, u32[]{:S(2)}) copy-start(f32[16,1280]{1,0:T(8,128)} %param.22) | copy-start | bytes 245764
  372.2 9.7 %copy-start.8 = (f32[1344]{0:T(1024)S(1)}, f32[1344]{0:T(1024)}, u32[]{:S(2)}) copy-start(f32[1344]{0:T(1024)} %param.24) | copy-start | bytes 16132
  372.2 9.7 %copy-start.9 = (f32[1344]{0:T(1024)S(1)}, f32[1344]{0:T(1024)}, u32[]{:S(2)}) copy-start(f32[1344]{0:T(1024)} %param.26) | copy-start | bytes 16132
  372.2 9.7 %copy-start.10 = (f32[1344]{0:T(1024)S(1)}, f32[1344]{0:T(1024)}, u32[]{:S(2)}) copy-start(f32[1344]{0:T(1024)} %param.25) | copy-start | bytes 16132
  376.7 13.8 %copy-start = (bf16[192,1280]{1,0:T(8,128)(2,1)}, bf16[192,1280]{1,0:T(8,128)(2,1)S(1)}, u32[]{:S(2)}) copy-start(bf16[192,1280]{1,0:T(8,128)(2,1)S(1)} %slice.29) | copy-start | bytes 1474564
  377.7 8.6 %all-to-all-start.1 = ((bf16[4,2,960]{2,1,0:T(2,128)(2,1)}), bf16[4,2,960]{2,1,0:T(2,128)(2,1)S(1)}, u32[]{:S(2)}, u32[]{:S(2)}) async-start(bf16[4,2,960]{2,1,0:T(2,128)(2,1)} %reshape.88), calls=%async_computation.1 | async-start | bytes 32768 | tf_op jit(solution)/shard_map/all_to_all | solution.py:15
  386.2 20.4 %all-to-all-start.2 = ((bf16[16,4,320]{2,0,1:T(8,128)(2,1)}), bf16[16,4,320]{2,0,1:T(8,128)(2,1)S(1)}, u32[]{:S(2)}, u32[]{:S(2)}) async-start(bf16[16,4,320]{2,0,1:T(8,128)(2,1)} %copy.60), calls=%async_computation.2 | async-start | bytes 98304 | tf_op jit(solution)/shard_map/all_to_all | solution.py:94
Sparse Core Ops, SparseCore 0:
  11.5 207.9 all-reduce.2
